TPU v7x, 256 devices: a whole 4x4x8 slice. The times are simulated.
256 devices in a mesh: section: 2 (over core), shard: 128 (over z, x, y).
Axes of the slice: x: 4, y: 4, z: 8, core: 2. Of those that a mesh axis runs over, the one named last changes fastest.
Arguments:
- hidden: bfloat16 [512, 32, 768], P('shard', None, 'section'), may hold values from -6 to 6
- proj: bfloat16 [768, 128], P('section'), may hold values from -0.21875 to 0.21875
- passages: bfloat16 [16384, 180, 128], P('shard'), may hold values from -24 to 24
- pass_len: int32 [16384], P('shard'), may hold values from 45 to 180
- query_len: int32 [512], P('shard'), may hold values from 8 to 32
- cand_owner: int32 [2, 512, 32, 1], P('section', 'shard'), may hold values from 0 to 127; in each aligned block of 128 rows (0 to 127, 128 to 255, ..., all dimensions but the last counted through in order) at most 2 rows name the same one
- cand_slot: int32 [2, 512, 32], P('section', 'shard'), may hold values from 0 to 127
- teacher: float32 [512, 64], P('shard', 'section'), may hold values from -18 to 318
Outputs:
- kl_div: float32 [512], P('shard')
- grad_hidden: bfloat16 [512, 32, 768], P('shard', None, 'section')
- grad_proj: float32 [768, 128], P('section')
Inputs may be any that keep to these rules, and one draw needn't show every extreme that they name: `cand_owner`: among the 128 candidates held by one device (one index of section, the queries of one index of shard), at most 2 name any one owner.
All inputs are finite; a program needn't handle non-finite values.
Results may differ from a plain program's by a relative error of at most 0.022.
Values may be sent and summed in bfloat16 or wider, within the bound.
No kernel may reach another device: no remote copies, remote signals or barrier semaphores. Data moves between devices by JAX's collectives and lax.ppermute only.
A program may use at most 128 MiB of HBM per device.

v0:
```python
import jax
import jax.numpy as jnp
from jax import lax
from jax.sharding import PartitionSpec as P

SHARPNESS = 64.0
EPSILON = 1e-06
NEGATIVE = -1e30


def combined_all(value, axis, join):
    pieces = jax.tree.map(lambda part: lax.all_gather(part, axis), value)
    head = jax.tree.map(lambda part: part[0], pieces)
    tail = jax.tree.map(lambda part: part[1:], pieces)
    running, _ = lax.scan(lambda running, section: (join(running, section), None), head, tail)
    return running


def token_scores(q_rows, blocks, cand_lens):
    logits = (
        jnp.einsum("bid,btd->bit", q_rows, blocks, preferred_element_type=jnp.float32) * SHARPNESS
    )
    in_range = jnp.arange(blocks.shape[1])[None, None, :] < cand_lens[:, None, None]
    logits = jnp.where(in_range, logits, NEGATIVE)
    top_logit = jnp.max(logits, axis=2, keepdims=True)
    expo_terms = jnp.where(in_range, jnp.exp(logits - top_logit), 0.0)
    total = jnp.sum(expo_terms, axis=2, keepdims=True)
    token_max = (top_logit[..., 0] + jnp.log(total[..., 0])) / SHARPNESS
    return (token_max, expo_terms / total)


def merge_halves(first, second):
    teach_top = jnp.maximum(first[0], second[0])
    scale_one = jnp.exp(first[0] - teach_top)
    scale_two = jnp.exp(second[0] - teach_top)
    stud_top = jnp.maximum(first[3], second[3])
    fact_one = jnp.exp(first[3] - stud_top)
    fact_two = jnp.exp(second[3] - stud_top)
    return (
        teach_top,
        first[1] * scale_one + second[1] * scale_two,
        first[2] * scale_one + second[2] * scale_two,
        stud_top,
        first[4] * fact_one + second[4] * fact_two,
    )


def local(hidden, proj, passages, pass_len, query_len, cand_owner, cand_slot, teacher):
    num_queries, num_tokens, feat_half = hidden.shape
    vec_dim = proj.shape[1]
    pass_tokens = passages.shape[1]
    owners = lax.axis_size("shard")
    flat_h = hidden.reshape(num_queries * num_tokens, feat_half)
    partial_in = jnp.dot(flat_h, proj, preferred_element_type=jnp.float32).reshape(
        num_queries, num_tokens, vec_dim
    )
    proj_in = lax.psum(partial_in, "section")
    inv_norm = lax.rsqrt(jnp.sum(proj_in * proj_in, axis=2, keepdims=True) + EPSILON)
    query_vecs = (proj_in * inv_norm).astype(jnp.bfloat16)
    tok_mask = jnp.arange(num_tokens)[None, :] < query_len[:, None]
    owner_ids = cand_owner.reshape(-1)
    slot_ids = cand_slot.reshape(-1)
    requests = owner_ids.shape[0]
    cand_half = requests // num_queries
    capacity = max(2, (2 * requests + owners - 1) // owners)
    onehot = (owner_ids[:, None] == jnp.arange(owners)[None, :]).astype(jnp.int32)
    rank_ids = jnp.sum((jnp.cumsum(onehot, axis=0) - onehot) * onehot, axis=1)
    buf_pos = owner_ids * capacity + rank_ids
    query_of = jnp.arange(requests) // cand_half
    req_mask = tok_mask[query_of]
    slot_table = jnp.zeros((owners, capacity), jnp.int32).at[owner_ids, rank_ids].set(slot_ids)
    wanted = lax.all_to_all(slot_table, "shard", split_axis=0, concat_axis=0, tiled=True).reshape(
        -1
    )
    out_blocks = passages[wanted].reshape(owners, capacity, pass_tokens, vec_dim)
    out_lens = pass_len[wanted].reshape(owners, capacity)
    got_blocks, got_lens = (
        lax.all_to_all(out_blocks, "shard", split_axis=0, concat_axis=0, tiled=True),
        lax.all_to_all(out_lens, "shard", split_axis=0, concat_axis=0, tiled=True),
    )
    blocks = got_blocks.reshape(owners * capacity, pass_tokens, vec_dim)[buf_pos]
    cand_lens = got_lens.reshape(-1)[buf_pos]
    token_max, weight = token_scores(query_vecs[query_of], blocks, cand_lens)
    student = jnp.sum(jnp.where(req_mask, token_max, 0.0), axis=1).reshape(num_queries, cand_half)
    teach_top = jnp.max(teacher, axis=1)
    teach_exp = jnp.exp(teacher - teach_top[:, None])
    teach_sum = jnp.sum(teach_exp, axis=1)
    teach_wsum = jnp.sum(teach_exp * (teacher - student), axis=1)
    stud_top = jnp.max(student, axis=1)
    stud_sum = jnp.sum(jnp.exp(student - stud_top[:, None]), axis=1)
    top_teach, sum_teach, wsum_teach, top_stud, sum_stud = combined_all(
        (teach_top, teach_sum, teach_wsum, stud_top, stud_sum), "section", merge_halves
    )
    lse_teach = top_teach + jnp.log(sum_teach)
    lse_stud = top_stud + jnp.log(sum_stud)
    kl_div = wsum_teach / sum_teach - lse_teach + lse_stud
    score_grad = jnp.exp(student - lse_stud[:, None]) - jnp.exp(teacher - lse_teach[:, None])
    flat_grad = score_grad.reshape(-1)
    mixed = jnp.where(req_mask[:, :, None], flat_grad[:, None, None] * weight, 0.0).astype(
        jnp.bfloat16
    )
    part_grad = jnp.einsum("bit,btd->bid", mixed, blocks, preferred_element_type=jnp.float32)
    half_grad = jnp.sum(part_grad.reshape(num_queries, cand_half, num_tokens, vec_dim), axis=1)
    vec_grad = lax.psum(half_grad, "section")
    cubed = inv_norm * inv_norm * inv_norm
    in_grad = inv_norm * vec_grad - cubed * proj_in * jnp.sum(
        proj_in * vec_grad, axis=2, keepdims=True
    )
    flat_in = in_grad.astype(jnp.bfloat16).reshape(num_queries * num_tokens, vec_dim)
    grad_hidden = jnp.dot(flat_in, proj.T, preferred_element_type=jnp.float32).astype(jnp.bfloat16)
    grad_hidden = grad_hidden.reshape(num_queries, num_tokens, feat_half)
    local_proj = jnp.dot(flat_h.T, flat_in, preferred_element_type=jnp.float32)
    grad_proj = lax.psum(local_proj, "shard")
    return (kl_div, grad_hidden, grad_proj)


def solution(mesh):
    in_specs = (
        P("shard", None, "section"),
        P("section", None),
        P("shard", None, None),
        P("shard"),
        P("shard"),
        P("section", "shard", None, None),
        P("section", "shard", None),
        P("shard", "section"),
    )
    out_specs = (P("shard"), P("shard", None, "section"), P("section", None))
    return jax.shard_map(local, mesh=mesh, in_specs=in_specs, out_specs=out_specs, check_vma=False)
```

profile of v0, /device:TPU:2, one launch (start us, length us, event | category | flops | bytes accessed | tf_op | source)
XLA Modules:
  0.0 680.3 jit_solution(7836206423100542883)
XLA Ops:
  7.2 0.8 eq.15
  8.0 0.1 fusion.7
  8.1 0.2 reduce_window_sum.11
  8.2 0.2 select_reduce_fusion.1
  8.4 0.5 broadcast.235
  8.9 1.3 reduce.11
  10.3 0.1 reshape.292
  10.4 0.8 reshape.352
  11.2 6.4 scatter_fusion
  17.5 0.1 copy.15
  17.6 26.6 %all_to_all.23 = s32[128,1,2]{2,1,0:T(1,128)S(1)} all-to-all(s32[128,1,2]{2,1,0:T(1,128)S(1)} %copy.15), channel_id=1, replica_groups=mesh['section'=2,'shard'=128] {'shard'}, dimensions={0} | all-to-all | bytes 2048 | tf_op jit(solution)/shard_map/all_to_all | solution.py:72
  44.2 0.8 reduce.12
  45.1 0.1 reshape.294
  45.2 1.9 gather_fusion.1
  47.1 0.8 all_to_all.17
  47.9 6.6 all-to-all-start.1
  54.5 44.5 %gather_fusion.4 = bf16[256,180,128]{2,0,1:T(8,128)(2,1)} fusion(bf16[128,180,128]{2,0,1:T(8,128)(2,1)} %param.10, s32[1024]{0:T(1024)S(1)} %pad_clamp_fusion.1), kind=kCustom, calls=%fused_computation.4 | custom fusion | bytes 23593984 | tf_op jit(solution)/shard_map/gather | solution.py:75
  99.0 11.2 %copy.17 = bf16[128,2,180,128]{3,1,2,0:T(2,128)(2,1)} copy(bf16[128,2,180,128]{3,1,0,2:T(2,128)(2,1)} %bitcast.41) | data formatting | bytes 23592960 | tf_op jit(solution)/shard_map/reshape | solution.py:75
  110.2 15.1 %all-to-all-start.2 = ((bf16[128,2,180,128]{3,1,2,0:T(2,128)(2,1)}), bf16[128,2,180,128]{3,1,2,0:T(2,128)(2,1)}, u32[]{:S(2)}, u32[]{:S(2)}) async-start(bf16[128,2,180,128]{3,1,2,0:T(2,128)(2,1)} %copy.17), calls=%async_computation.2 | async-start | bytes 23592960 | tf_op jit(solution)/shard_map/all_to_all | solution.py:78
  125.4 0.0 all-reduce.10.cloned.1.call-start
  125.5 0.8 fusion.5
  126.3 0.0 all-reduce.10.cloned.1.call-update
  126.3 0.0 all-reduce.12.cloned.1.call-start
  126.4 0.1 iota_compare_fusion.2
  126.5 0.7 gather_fusion
  127.2 0.1 reduce_max.27
  127.3 0.6 dynamic-slice
  128.5 0.2 dynamic-update-slice.1
  128.8 0.8 reduce.13
  129.6 0.1 reshape.295
  129.7 1.3 gather_fusion.2
  131.0 0.1 iota_compare_fusion
  131.1 28.1 %all-reduce.10.cloned.1.call-done = f32[4,32,128]{2,1,0:T(8,128)} async-done(((f32[4,32,128]{2,1,0:T(8,128)}), f32[4,32,128]{2,1,0:T(8,128)}) %all-reduce.10.cloned.1.call-update) | async-done | bytes 65552 | tf_op jit(solution)/shard_map/psum | solution.py:57
  159.2 0.9 multiply_reduce_fusion.1
  160.1 0.9 multiply_convert_fusion
  161.0 0.8 gather_fusion.3
  161.8 219.7 %all-to-all-done.2 = bf16[128,2,180,128]{3,1,2,0:T(2,128)(2,1)} async-done(((bf16[128,2,180,128]{3,1,2,0:T(2,128)(2,1)}), bf16[128,2,180,128]{3,1,2,0:T(2,128)(2,1)}, u32[]{:S(2)}, u32[]{:S(2)}) %all-to-all-start.2) | async-done | bytes 11796512 | tf_op jit(solution)/shard_map/all_to_all | solution.py:78
  381.5 11.3 %copy.18 = bf16[128,2,180,128]{3,2,1,0:T(8,128)(2,1)} copy(bf16[128,2,180,128]{3,1,2,0:T(2,128)(2,1)} %all-to-all-done.2) | data formatting | bytes 23592960 | tf_op jit(solution)/shard_map/all_to_all | solution.py:78
  392.8 8.3 %gather_fusion.5 = bf16[128,180,128]{2,1,0:T(8,128)(2,1)} fusion(bf16[256,180,128]{2,1,0:T(8,128)(2,1)} %bitcast.42, s32[1024]{0:T(1024)S(1)} %pad_clamp_fusion), kind=kCustom, calls=%fused_computation.5 | custom fusion | bytes 11796992 | tf_op jit(solution)/shard_map/gather | solution.py:81
  401.1 6.6 fusion
  407.8 1.9 copy-done.1
  409.7 1.8 fusion.1
  411.5 0.1 select_reduce_fusion
  411.6 0.1 reshape.298
  411.7 0.1 reduce_max.29
  411.8 0.2 multiply_reduce_fusion.2
  412.1 0.2 dynamic-update-slice.3
  412.3 0.2 dynamic-update-slice
  412.5 0.2 dynamic-update-slice.2
  412.7 0.2 dynamic-update-slice.4
  412.9 2.4 all-reduce.5
  415.4 0.6 subtract_add_fusion
  416.0 0.1 exponential_subtract_fusion
  416.1 0.1 mul.138
  416.2 6.0 bitcast_reduce_fusion
  422.1 0.0 all-reduce.12.cloned.1.call-update
  422.2 0.0 all-reduce.14.cloned.1.call-start
  422.2 27.8 %all-reduce.12.cloned.1.call-done = f32[4,32,128]{2,1,0:T(8,128)} async-done(((f32[4,32,128]{2,1,0:T(8,128)}), f32[4,32,128]{2,1,0:T(8,128)}) %all-reduce.12.cloned.1.call-update) | async-done | bytes 65552 | tf_op jit(solution)/shard_map/psum | solution.py:104
  450.0 0.9 multiply_reduce_fusion
  451.0 1.0 subtract_convert_fusion
  451.9 0.9 convolution_bitcast_fusion
  452.8 0.8 convolution_convert_fusion
  453.7 218.4 %all-reduce.14.cloned.1.call-done = f32[384,128]{0,1:T(8,128)} async-done(((f32[384,128]{0,1:T(8,128)}), f32[384,128]{0,1:T(8,128)}) %all-reduce.14.cloned.1.call-update) | async-done | bytes 196624 | tf_op jit(solution)/shard_map/psum | solution.py:113
  672.1 1.7 copy.19
  (28 shorter events, 0.1 us)
Async XLA Ops:
  7.2 118.3 %copy-start = (bf16[4,32,384]{2,1,0:T(8,128)(2,1)S(1)}, bf16[4,32,384]{2,1,0:T(8,128)(2,1)}, u32[]{:S(2)}) copy-start(bf16[4,32,384]{2,1,0:T(8,128)(2,1)} %param.8) | copy-start | bytes 294916
  47.9 62.3 %all-to-all-start.1 = ((s32[128,1,2]{2,1,0:T(1,128)}), s32[128,1,2]{2,1,0:T(1,128)S(1)}, u32[]{:S(2)}, u32[]{:S(2)}) async-start(s32[128,1,2]{2,1,0:T(1,128)} %bitcast.5), calls=%async_computation.1 | async-start | bytes 131072 | tf_op jit(solution)/shard_map/all_to_all | solution.py:79
  110.2 15.3 %copy-start.3 = (bf16[384,128]{1,0:T(8,128)(2,1)S(1)}, bf16[384,128]{1,0:T(8,128)(2,1)}, u32[]{:S(2)}) copy-start(bf16[384,128]{1,0:T(8,128)(2,1)} %param.9) | copy-start | bytes 294916
  110.2 16.2 %copy-start.5 = (s32[4]{0:T(128)S(1)}, s32[4]{0:T(128)}, u32[]{:S(2)}) copy-start(s32[4]{0:T(128)} %param.12) | copy-start | bytes 52
  110.2 16.9 %copy-start.4 = (f32[4,32]{1,0:T(4,128)S(1)}, f32[4,32]{1,0:T(4,128)}, u32[]{:S(2)}) copy-start(f32[4,32]{1,0:T(4,128)} %param.15) | copy-start | bytes 1540
  110.2 17.1 %copy-start.6 = (u32[256]{0:T(256)S(1)}, u32[256]{0:T(256)}, u32[]{:S(2)}) copy-start(u32[256]{0:T(256)} %constant.81) | copy-start | bytes 3076
  110.2 271.3 %all-to-all-start.2 = ((bf16[128,2,180,128]{3,1,2,0:T(2,128)(2,1)}), bf16[128,2,180,128]{3,1,2,0:T(2,128)(2,1)}, u32[]{:S(2)}, u32[]{:S(2)}) async-start(bf16[128,2,180,128]{3,1,2,0:T(2,128)(2,1)} %copy.17), calls=%async_computation.2 | async-start | bytes 23592960 | tf_op jit(solution)/shard_map/all_to_all | solution.py:78
  125.4 33.8 %all-reduce.10.cloned.1.call-start = ((), (), s32[]{:S(2)}) async-start(), calls=%async_computation.3 | async-start | bytes 131072 | tf_op jit(solution)/shard_map/psum | solution.py:57
  126.3 323.7 %all-reduce.12.cloned.1.call-start = ((), (), s32[]{:S(2)}) async-start(), calls=%async_computation.4 | async-start | bytes 131072 | tf_op jit(solution)/shard_map/psum | solution.py:104
  407.8 1.9 copy-start.1
  416.1 33.9 %copy-start.2 = (f32[4,32,128]{2,1,0:T(8,128)S(1)}, f32[4,32,128]{2,1,0:T(8,128)}, u32[]{:S(2)}) copy-start(f32[4,32,128]{2,1,0:T(8,128)} %all-reduce.10.cloned.1.call-done) | copy-start | bytes 196612
  422.2 249.9 %all-reduce.14.cloned.1.call-start = ((), (), s32[]{:S(2)}) async-start(), calls=%async_computation.5 | async-start | bytes 393216 | tf_op jit(solution)/shard_map/psum | solution.py:113
Sparse Core Ops, SparseCore 0:
  129.3 29.8 all-reduce.9
  422.3 27.6 all-reduce.11
  456.1 215.9 all-reduce.13
where the time goes:
time: 681 us; the launch traced here: 680 us
  waiting for transfers between devices  494 us (73%)
  local copies, waits for them, and re-layouts  95.1 us (14%)
  blocking collectives  29 us (4%)
  starting transfers between devices  21.9 us (3%)
  matrix products  15.1 us (2%)
  between operations  14.7 us (2%)
  other arithmetic  10.4 us (2%)
    all_to_all x1, waiting for transfers between devices, local(): lax.all_to_all(out_blocks, 'shard', split_axis=0, concat_axis=0, tiled=True)  220 us
    psum x1, waiting for transfers between devices, local(): grad_proj = lax.psum(local_proj, 'shard')  218 us
    gather x1, local copies, waits for them, and re-layouts, local(): passages[wanted].reshape(owners, capacity, pass_tokens, vec_dim)  44.5 us
    psum x1, waiting for transfers between devices, local(): proj_in = lax.psum(partial_in, 'section')  28.1 us
    psum x1, waiting for transfers between devices, local(): vec_grad = lax.psum(half_grad, 'section')  27.8 us
    all_to_all x1, blocking collectives, local(): lax.all_to_all(slot_table, 'shard', split_axis=0, concat_axis=0, tiled=True)  26.6 us
    all_to_all x1, starting transfers between devices, local(): lax.all_to_all(out_blocks, 'shard', split_axis=0, concat_axis=0, tiled=True)  15.1 us
  transfers between devices with their start and end apart: 5, of which 4 were waited for; matrix products, arithmetic and copies ran while one was open for 9% of the time, Pallas kernels for 0%

commit v1 on v0

--- a/solution.py
+++ b/solution.py
@@ -45,6 +45,17 @@
     )
 
 
+def pair_sum(value):
+    return value + lax.ppermute(value, "section", [(0, 1), (1, 0)])
+
+
+def spread_sum(value, axis, size):
+    pieces = value.reshape(size, -1, value.shape[-1])
+    summed = lax.all_to_all(pieces, axis, 0, 0, tiled=True).sum(axis=0)
+    spread = jnp.broadcast_to(summed[None], pieces.shape)
+    return lax.all_to_all(spread, axis, 0, 0, tiled=True).reshape(value.shape)
+
+
 def local(hidden, proj, passages, pass_len, query_len, cand_owner, cand_slot, teacher):
     num_queries, num_tokens, feat_half = hidden.shape
     vec_dim = proj.shape[1]
@@ -54,7 +65,7 @@
     partial_in = jnp.dot(flat_h, proj, preferred_element_type=jnp.float32).reshape(
         num_queries, num_tokens, vec_dim
     )
-    proj_in = lax.psum(partial_in, "section")
+    proj_in = pair_sum(partial_in)
     inv_norm = lax.rsqrt(jnp.sum(proj_in * proj_in, axis=2, keepdims=True) + EPSILON)
     query_vecs = (proj_in * inv_norm).astype(jnp.bfloat16)
     tok_mask = jnp.arange(num_tokens)[None, :] < query_len[:, None]
@@ -101,7 +112,7 @@
     )
     part_grad = jnp.einsum("bit,btd->bid", mixed, blocks, preferred_element_type=jnp.float32)
     half_grad = jnp.sum(part_grad.reshape(num_queries, cand_half, num_tokens, vec_dim), axis=1)
-    vec_grad = lax.psum(half_grad, "section")
+    vec_grad = pair_sum(half_grad)
     cubed = inv_norm * inv_norm * inv_norm
     in_grad = inv_norm * vec_grad - cubed * proj_in * jnp.sum(
         proj_in * vec_grad, axis=2, keepdims=True
@@ -110,7 +121,7 @@
     grad_hidden = jnp.dot(flat_in, proj.T, preferred_element_type=jnp.float32).astype(jnp.bfloat16)
     grad_hidden = grad_hidden.reshape(num_queries, num_tokens, feat_half)
     local_proj = jnp.dot(flat_h.T, flat_in, preferred_element_type=jnp.float32)
-    grad_proj = lax.psum(local_proj, "shard")
+    grad_proj = spread_sum(local_proj, "shard", owners)
     return (kl_div, grad_hidden, grad_proj)
 
 

time: 681 us -> 467 us (0.69)
  waiting for transfers between devices: 494 us -> 265 us
  blocking collectives: 29 us -> 55.7 us
  between operations: 14.7 us -> 1.62 us
  starting transfers between devices: 21.9 us -> 29.2 us
    psum x3 -> x0, waiting for transfers between devices: 274 us -> none  [the longest x1 218 us: local(): grad_proj = lax.psum(local_proj, 'shard')]
    all_to_all x1, waiting for transfers between devices: 220 us -> 251 us  [local(): lax.all_to_all(out_blocks, 'shard', split_axis=0, concat_axis=0, tiled=True)]
    all_to_all x0 -> x1, blocking collectives: none -> 26.7 us  [spread_sum(): summed = lax.all_to_all(pieces, axis, 0, 0, tiled=True).sum(axis=0)]
    all_to_all x0 -> x1, waiting for transfers between devices: none -> 12.5 us  [spread_sum(): return lax.all_to_all(spread, axis, 0, 0, tiled=True).reshape(value.shape)]
  transfers between devices with their start and end apart: 5 -> 5, of which waited for: 4 -> 3; matrix products, arithmetic and copies ran while one was open for 9% -> 13% of each run, Pallas kernels for 0% -> 0%
where the time goes in v1:
time: 467 us
  waiting for transfers between devices  265 us (57%)
  local copies, waits for them, and re-layouts  95.1 us (20%)
  blocking collectives  55.7 us (12%)
  starting transfers between devices  29.2 us (6%)
  matrix products  13.2 us (3%)
  other arithmetic  7.22 us (2%)
    all_to_all x1, waiting for transfers between devices, local(): lax.all_to_all(out_blocks, 'shard', split_axis=0, concat_axis=0, tiled=True)  251 us
    gather x1, local copies, waits for them, and re-layouts, local(): passages[wanted].reshape(owners, capacity, pass_tokens, vec_dim)  44.5 us
    all_to_all x1, blocking collectives, spread_sum(): summed = lax.all_to_all(pieces, axis, 0, 0, tiled=True).sum(axis=0)  26.7 us
    all_to_all x1, blocking collectives, local(): lax.all_to_all(slot_table, 'shard', split_axis=0, concat_axis=0, tiled=True)  26.6 us
    all_to_all x1, starting transfers between devices, local(): lax.all_to_all(out_blocks, 'shard', split_axis=0, concat_axis=0, tiled=True)  15.4 us
    all_to_all x1, waiting for transfers between devices, spread_sum(): return lax.all_to_all(spread, axis, 0, 0, tiled=True).reshape(value.shape)  12.5 us
    all_to_all x1, local copies, waits for them, and re-layouts, local(): lax.all_to_all(out_blocks, 'shard', split_axis=0, concat_axis=0, tiled=True)  11.3 us
    reshape x1, local copies, waits for them, and re-layouts, local(): passages[wanted].reshape(owners, capacity, pass_tokens, vec_dim)  11.2 us
  transfers between devices with their start and end apart: 5, of which 3 were waited for; matrix products, arithmetic and copies ran while one was open for 13% of the time, Pallas kernels for 0%

profile of v1, /device:TPU:2, one launch (start us, length us, event | category | flops | bytes accessed | tf_op | source)
XLA Modules:
  0.0 466.7 jit_solution(15689764057543353158)
XLA Ops:
  0.6 0.8 eq.15
  1.4 0.1 fusion.7
  1.5 0.2 reduce_window_sum.11
  1.7 0.2 select_reduce_fusion.1
  1.9 0.5 broadcast.236
  2.4 1.3 reduce.11
  3.8 0.1 reshape.299
  3.8 0.8 reshape.361
  4.6 6.4 %scatter_fusion = s32[128,2]{0,1:T(2,128)S(1)} fusion(s32[128,2]{0,1:T(2,128)S(1)} %broadcast_in_dim.32, s32[128]{0:T(128)S(1)} %get-tuple-element.52, s32[128]{0:T(128)S(1)} %reshape.361), kind=kCustom, calls=%fused_computation.6 | custom fusion | bytes 2560 | tf_op jit(solution)/shard_map/scatter | solution.py:82
  11.0 0.1 copy.14
  11.1 26.6 %all_to_all.33 = s32[128,1,2]{2,1,0:T(1,128)S(1)} all-to-all(s32[128,1,2]{2,1,0:T(1,128)S(1)} %copy.14), channel_id=1, replica_groups=mesh['section'=2,'shard'=128] {'shard'}, dimensions={0} | all-to-all | bytes 2048 | tf_op jit(solution)/shard_map/all_to_all | solution.py:83
  37.7 0.8 reduce.12
  38.5 0.1 reshape.301
  38.7 1.9 gather_fusion.1
  40.6 0.8 all_to_all.23
  41.4 6.6 %all-to-all-start.1 = ((s32[128,1,2]{2,1,0:T(1,128)}), s32[128,1,2]{2,1,0:T(1,128)S(1)}, u32[]{:S(2)}, u32[]{:S(2)}) async-start(s32[128,1,2]{2,1,0:T(1,128)} %bitcast.5), calls=%async_computation.1 | async-start | bytes 131072 | tf_op jit(solution)/shard_map/all_to_all | solution.py:90
  48.0 44.5 %gather_fusion.4 = bf16[256,180,128]{2,0,1:T(8,128)(2,1)} fusion(bf16[128,180,128]{2,0,1:T(8,128)(2,1)} %param.10, s32[1024]{0:T(1024)S(1)} %pad_clamp_fusion.1), kind=kCustom, calls=%fused_computation.4 | custom fusion | bytes 23593984 | tf_op jit(solution)/shard_map/gather | solution.py:86
  92.5 11.2 %copy.16 = bf16[128,2,180,128]{3,1,2,0:T(2,128)(2,1)} copy(bf16[128,2,180,128]{3,1,0,2:T(2,128)(2,1)} %bitcast.41) | data formatting | bytes 23592960 | tf_op jit(solution)/shard_map/reshape | solution.py:86
  103.7 15.4 %all-to-all-start.2 = ((bf16[128,2,180,128]{3,1,2,0:T(2,128)(2,1)}), bf16[128,2,180,128]{3,1,2,0:T(2,128)(2,1)}, u32[]{:S(2)}, u32[]{:S(2)}) async-start(bf16[128,2,180,128]{3,1,2,0:T(2,128)(2,1)} %copy.16), calls=%async_computation.2 | async-start | bytes 23592960 | tf_op jit(solution)/shard_map/all_to_all | solution.py:89
  119.1 0.2 fusion.5
  119.3 0.1 collective-permute-start
  119.5 0.7 gather_fusion
  120.2 0.1 reduce_max.27
  120.3 0.6 dynamic-slice
  121.6 0.2 dynamic-update-slice.1
  121.8 0.8 reduce.13
  122.7 0.1 reshape.302
  122.8 1.3 gather_fusion.2
  124.1 0.1 iota_compare_fusion
  124.2 0.1 multiply_reduce_fusion.1
  124.3 0.1 multiply_convert_fusion
  124.4 0.8 gather_fusion.3
  125.1 251.0 %all-to-all-done.2 = bf16[128,2,180,128]{3,1,2,0:T(2,128)(2,1)} async-done(((bf16[128,2,180,128]{3,1,2,0:T(2,128)(2,1)}), bf16[128,2,180,128]{3,1,2,0:T(2,128)(2,1)}, u32[]{:S(2)}, u32[]{:S(2)}) %all-to-all-start.2) | async-done | bytes 11796512 | tf_op jit(solution)/shard_map/all_to_all | solution.py:89
  376.2 11.3 %copy.17 = bf16[128,2,180,128]{3,2,1,0:T(8,128)(2,1)} copy(bf16[128,2,180,128]{3,1,2,0:T(2,128)(2,1)} %all-to-all-done.2) | data formatting | bytes 23592960 | tf_op jit(solution)/shard_map/all_to_all | solution.py:89
  387.5 8.3 %gather_fusion.5 = bf16[128,180,128]{2,1,0:T(8,128)(2,1)} fusion(bf16[256,180,128]{2,1,0:T(8,128)(2,1)} %bitcast.42, s32[1024]{0:T(1024)S(1)} %pad_clamp_fusion), kind=kCustom, calls=%fused_computation.5 | custom fusion | bytes 11796992 | tf_op jit(solution)/shard_map/gather | solution.py:92
  395.8 6.6 %fusion = (f32[128,32]{1,0:T(8,128)S(1)}, f32[128,32,180]{2,1,0:T(8,128)S(1)}) fusion(pred[128,180]{1,0:T(8,128)(4,1)S(1)} %iota_compare_fusion, bf16[128,32,128]{2,1,0:T(8,128)(2,1)S(1)} %gather_fusion.3, bf16[128,180,128]{2,1,0:T(8,128)(2,1)} %gather_fusion.5), kind=kOutput, calls=%fused_computation.10 | convolution fusion | flops 190951424 | bytes 9935360 | tf_op jit(solution)/shard_map/bid,btd->bit/dot_general | solution.py:21
  402.4 1.9 copy-done.1
  404.3 1.8 fusion.1
  406.2 0.1 select_reduce_fusion
  406.3 0.1 reshape.305
  406.4 0.1 reduce_max.29
  406.5 0.2 multiply_reduce_fusion.2
  406.7 0.2 dynamic-update-slice.3
  407.0 0.2 dynamic-update-slice
  407.2 0.2 dynamic-update-slice.2
  407.4 0.2 dynamic-update-slice.4
  407.6 2.4 all-reduce.5
  410.0 0.6 subtract_add_fusion
  410.7 0.1 mul.138
  410.8 5.3 %bitcast_reduce_fusion = f32[4,32,128]{2,1,0:T(8,128)S(1)} fusion(bf16[128,180,128]{2,1,0:T(8,128)(2,1)} %gather_fusion.5, f32[128,32,180]{2,1,0:T(8,128)} %copy-done.1, f32[128,32]{1,0:T(8,128)S(1)} %fusion.1, f32[128]{0:T(128)S(1)} %mul.138, f32[128,32]{1,0:T(8,128)S(1)} %get-tuple-element.53, pred[128,32]{1,0:T(8,128)(4,1)S(1)} %gather_fusion, ...), kind=kOutput, calls=%fused_computation.12 | convolution fusion | flops 195149824 | bytes 8973312 | tf_op jit(solution)/shard_map/bit,btd->bid/dot_general | solution.py:113
  416.1 0.5 collective-permute-start.1
  416.7 1.1 collective-permute-done.1
  417.7 0.1 multiply_reduce_fusion
  417.8 0.1 subtract_convert_fusion
  418.0 0.2 convolution_bitcast_fusion
  418.2 0.1 copy.18
  418.3 0.1 reshape.309
  418.4 26.7 %all_to_all.34 = f32[128,3,128]{2,1,0:T(4,128)S(1)} all-to-all(f32[128,3,128]{2,1,0:T(4,128)S(1)} %reshape.309), channel_id=1, replica_groups=mesh['section'=2,'shard'=128] {'shard'}, dimensions={0} | all-to-all | bytes 393216 | tf_op jit(solution)/shard_map/all_to_all | solution.py:54
  445.1 0.1 reduce_sum.102
  445.2 0.7 broadcast_in_dim.42
  445.9 6.6 %all-to-all-start.4 = ((f32[128,3,128]{2,1,0:T(4,128)}), f32[128,3,128]{2,1,0:T(4,128)S(1)}, u32[]{:S(2)}, u32[]{:S(2)}) async-start(f32[128,3,128]{2,1,0:T(4,128)} %broadcast_in_dim.42), calls=%async_computation.4 | async-start | bytes 524288 | tf_op jit(solution)/shard_map/all_to_all | solution.py:56
  452.6 0.8 convolution_convert_fusion
  453.4 12.5 %all-to-all-done.4 = f32[128,3,128]{2,1,0:T(4,128)S(1)} async-done(((f32[128,3,128]{2,1,0:T(4,128)}), f32[128,3,128]{2,1,0:T(4,128)S(1)}, u32[]{:S(2)}, u32[]{:S(2)}) %all-to-all-start.4) | async-done | bytes 196640 | tf_op jit(solution)/shard_map/all_to_all | solution.py:56
  465.9 0.8 reshape.310
  (28 shorter events, 0.2 us)
Async XLA Ops:
  0.6 118.5 %copy-start = (bf16[4,32,384]{2,1,0:T(8,128)(2,1)S(1)}, bf16[4,32,384]{2,1,0:T(8,128)(2,1)}, u32[]{:S(2)}) copy-start(bf16[4,32,384]{2,1,0:T(8,128)(2,1)} %param.8) | copy-start | bytes 294916
  41.4 62.3 %all-to-all-start.1 = ((s32[128,1,2]{2,1,0:T(1,128)}), s32[128,1,2]{2,1,0:T(1,128)S(1)}, u32[]{:S(2)}, u32[]{:S(2)}) async-start(s32[128,1,2]{2,1,0:T(1,128)} %bitcast.5), calls=%async_computation.1 | async-start | bytes 131072 | tf_op jit(solution)/shard_map/all_to_all | solution.py:90
  103.6 15.5 %copy-start.2 = (bf16[384,128]{1,0:T(8,128)(2,1)S(1)}, bf16[384,128]{1,0:T(8,128)(2,1)}, u32[]{:S(2)}) copy-start(bf16[384,128]{1,0:T(8,128)(2,1)} %param.9) | copy-start | bytes 294916
  103.6 15.8 %copy-start.4 = (s32[4]{0:T(128)S(1)}, s32[4]{0:T(128)}, u32[]{:S(2)}) copy-start(s32[4]{0:T(128)} %param.12) | copy-start | bytes 52
  103.7 16.6 %copy-start.3 = (f32[4,32]{1,0:T(4,128)S(1)}, f32[4,32]{1,0:T(4,128)}, u32[]{:S(2)}) copy-start(f32[4,32]{1,0:T(4,128)} %param.15) | copy-start | bytes 1540
  103.7 16.7 %copy-start.5 = (u32[256]{0:T(256)S(1)}, u32[256]{0:T(256)}, u32[]{:S(2)}) copy-start(u32[256]{0:T(256)} %constant.81) | copy-start | bytes 3076
  103.7 272.5 %all-to-all-start.2 = ((bf16[128,2,180,128]{3,1,2,0:T(2,128)(2,1)}), bf16[128,2,180,128]{3,1,2,0:T(2,128)(2,1)}, u32[]{:S(2)}, u32[]{:S(2)}) async-start(bf16[128,2,180,128]{3,1,2,0:T(2,128)(2,1)} %copy.16), calls=%async_computation.2 | async-start | bytes 23592960 | tf_op jit(solution)/shard_map/all_to_all | solution.py:89
  119.3 4.9 %collective-permute-start = (f32[4,32,128]{2,1,0:T(8,128)S(1)}, f32[4,32,128]{2,1,0:T(8,128)S(1)}, u32[]{:S(2)}, u32[]{:S(2)}) collective-permute-start(f32[4,32,128]{2,1,0:T(8,128)S(1)} %fusion.5), channel_id=1, source_target_pairs={{0,128},{128,0},{1,129},{129,1},{2,130},{130,2},{3,131},{131,3},{4... | collective-permute-start | bytes 196616 | tf_op jit(solution)/shard_map/ppermute | solution.py:49
  402.4 1.9 copy-start.1
  416.1 1.6 collective-permute-start.1
  445.9 19.9 %all-to-all-start.4 = ((f32[128,3,128]{2,1,0:T(4,128)}), f32[128,3,128]{2,1,0:T(4,128)S(1)}, u32[]{:S(2)}, u32[]{:S(2)}) async-start(f32[128,3,128]{2,1,0:T(4,128)} %broadcast_in_dim.42), calls=%async_computation.4 | async-start | bytes 524288 | tf_op jit(solution)/shard_map/all_to_all | solution.py:56

commit v2 on v1

--- a/solution.py
+++ b/solution.py
@@ -6,6 +6,7 @@
 SHARPNESS = 64.0
 EPSILON = 1e-06
 NEGATIVE = -1e30
+CAPACITY = 2
 
 
 def combined_all(value, axis, join):
@@ -56,10 +57,25 @@
     return lax.all_to_all(spread, axis, 0, 0, tiled=True).reshape(value.shape)
 
 
+def split_three(value):
+    high = lax.reduce_precision(value, exponent_bits=8, mantissa_bits=7)
+    rest = value - high
+    middle = lax.reduce_precision(rest, exponent_bits=8, mantissa_bits=7)
+    return high, middle, rest - middle
+
+
+def lane_row(width, entries):
+    lane = jnp.arange(width)[None, :]
+    row = jnp.zeros((entries[0].shape[0], width), jnp.float32)
+    for place, entry in enumerate(entries):
+        row = jnp.where(lane == place, entry.astype(jnp.float32)[:, None], row)
+    return row.astype(jnp.bfloat16)
+
+
 def local(hidden, proj, passages, pass_len, query_len, cand_owner, cand_slot, teacher):
     num_queries, num_tokens, feat_half = hidden.shape
     vec_dim = proj.shape[1]
-    pass_tokens = passages.shape[1]
+    held, pass_tokens = passages.shape[0], passages.shape[1]
     owners = lax.axis_size("shard")
     flat_h = hidden.reshape(num_queries * num_tokens, feat_half)
     partial_in = jnp.dot(flat_h, proj, preferred_element_type=jnp.float32).reshape(
@@ -73,26 +89,58 @@
     slot_ids = cand_slot.reshape(-1)
     requests = owner_ids.shape[0]
     cand_half = requests // num_queries
-    capacity = max(2, (2 * requests + owners - 1) // owners)
+    capacity = CAPACITY
+    slots = owners * capacity
     onehot = (owner_ids[:, None] == jnp.arange(owners)[None, :]).astype(jnp.int32)
     rank_ids = jnp.sum((jnp.cumsum(onehot, axis=0) - onehot) * onehot, axis=1)
     buf_pos = owner_ids * capacity + rank_ids
     query_of = jnp.arange(requests) // cand_half
-    req_mask = tok_mask[query_of]
-    slot_table = jnp.zeros((owners, capacity), jnp.int32).at[owner_ids, rank_ids].set(slot_ids)
-    wanted = lax.all_to_all(slot_table, "shard", split_axis=0, concat_axis=0, tiled=True).reshape(
-        -1
+    pick = buf_pos[None, :] == jnp.arange(slots)[:, None]
+    slot_query = jnp.any(pick[:, :, None] & (query_of[:, None] == jnp.arange(num_queries))[None], axis=1)
+    row = num_tokens * vec_dim
+    q_send = jnp.dot(
+        slot_query.astype(jnp.bfloat16),
+        query_vecs.reshape(num_queries, row),
+        preferred_element_type=jnp.float32,
+    ).astype(jnp.bfloat16)
+    slot_meta = jnp.sum(jnp.where(pick, slot_ids[None, :], 0), axis=1)
+    qlen_meta = jnp.sum(jnp.where(pick, query_len[query_of][None, :], 0), axis=1)
+    width = row + vec_dim
+    payload = jnp.concatenate([q_send, lane_row(vec_dim, (slot_meta, qlen_meta))], axis=1)
+    recv = lax.all_to_all(
+        payload.reshape(owners, capacity * width), "shard", 0, 0, tiled=True
+    ).reshape(slots, width)
+    q_rows = recv[:, :row].reshape(slots, num_tokens, vec_dim)
+    slot_at = recv[:, row].astype(jnp.int32)
+    qlen_at = recv[:, row + 1].astype(jnp.int32)
+    choose = slot_at[:, None] == jnp.arange(held)[None, :]
+    blocks = (
+        jnp.dot(
+            choose.astype(jnp.bfloat16),
+            passages.reshape(held, pass_tokens * vec_dim),
+            preferred_element_type=jnp.float32,
+        )
+        .astype(jnp.bfloat16)
+        .reshape(slots, pass_tokens, vec_dim)
     )
-    out_blocks = passages[wanted].reshape(owners, capacity, pass_tokens, vec_dim)
-    out_lens = pass_len[wanted].reshape(owners, capacity)
-    got_blocks, got_lens = (
-        lax.all_to_all(out_blocks, "shard", split_axis=0, concat_axis=0, tiled=True),
-        lax.all_to_all(out_lens, "shard", split_axis=0, concat_axis=0, tiled=True),
+    cand_lens = jnp.sum(jnp.where(choose, pass_len[None, :], 0), axis=1)
+    token_max, weight = token_scores(q_rows, blocks, cand_lens)
+    stud_at = jnp.sum(
+        jnp.where(jnp.arange(num_tokens)[None, :] < qlen_at[:, None], token_max, 0.0), axis=1
     )
-    blocks = got_blocks.reshape(owners * capacity, pass_tokens, vec_dim)[buf_pos]
-    cand_lens = got_lens.reshape(-1)[buf_pos]
-    token_max, weight = token_scores(query_vecs[query_of], blocks, cand_lens)
-    student = jnp.sum(jnp.where(req_mask, token_max, 0.0), axis=1).reshape(num_queries, cand_half)
+    pulled = jnp.einsum(
+        "bit,btd->bid", weight.astype(jnp.bfloat16), blocks, preferred_element_type=jnp.float32
+    )
+    back = jnp.concatenate(
+        [pulled.astype(jnp.bfloat16).reshape(slots, row), lane_row(vec_dim, split_three(stud_at))],
+        axis=1,
+    )
+    got = lax.all_to_all(
+        back.reshape(owners, capacity * width), "shard", 0, 0, tiled=True
+    ).reshape(slots, width)
+    mine = jnp.dot(pick.T.astype(jnp.bfloat16), got, preferred_element_type=jnp.float32)
+    student = ((mine[:, row] + mine[:, row + 1]) + mine[:, row + 2]).reshape(num_queries, cand_half)
+    pulled_mine = mine[:, :row].reshape(num_queries, cand_half, num_tokens, vec_dim)
     teach_top = jnp.max(teacher, axis=1)
     teach_exp = jnp.exp(teacher - teach_top[:, None])
     teach_sum = jnp.sum(teach_exp, axis=1)
@@ -106,12 +154,8 @@
     lse_stud = top_stud + jnp.log(sum_stud)
     kl_div = wsum_teach / sum_teach - lse_teach + lse_stud
     score_grad = jnp.exp(student - lse_stud[:, None]) - jnp.exp(teacher - lse_teach[:, None])
-    flat_grad = score_grad.reshape(-1)
-    mixed = jnp.where(req_mask[:, :, None], flat_grad[:, None, None] * weight, 0.0).astype(
-        jnp.bfloat16
-    )
-    part_grad = jnp.einsum("bit,btd->bid", mixed, blocks, preferred_element_type=jnp.float32)
-    half_grad = jnp.sum(part_grad.reshape(num_queries, cand_half, num_tokens, vec_dim), axis=1)
+    half_grad = jnp.sum(score_grad[:, :, None, None] * pulled_mine, axis=1)
+    half_grad = jnp.where(tok_mask[:, :, None], half_grad, 0.0)
     vec_grad = pair_sum(half_grad)
     cubed = inv_norm * inv_norm * inv_norm
     in_grad = inv_norm * vec_grad - cubed * proj_in * jnp.sum(

time: 467 us -> 374 us (0.80); the launches traced: 467 us -> 367 us
  waiting for transfers between devices: 265 us -> 111 us
  other arithmetic: 7.22 us -> 73.2 us
  blocking collectives: 55.7 us -> 24.3 us
  matrix products: 13.2 us -> 33.9 us
    all_to_all x2, waiting for transfers between devices: 251 us -> 97.5 us  [the longest x1 52 us: local(): lax.all_to_all(back.reshape(owners, capacity * width), 'shard', 0, 0, til...]
    gather x6 -> x1, local copies, waits for them, and re-layouts: 57.4 us -> 1.47 us  [local(): query_len[query_of][None, :]]
    all_to_all x2 -> x4, other arithmetic: 1.61 us -> 55.1 us  [the longest x2 28.2 us: local(): lax.all_to_all(payload.reshape(owners, capacity * width), 'shard', 0, 0,...]
    unnamed x24 -> x42, local copies, waits for them, and re-layouts: 4.15 us -> 35.7 us
    all_to_all x1 -> x0, blocking collectives: 26.6 us -> none  [local(): lax.all_to_all(slot_table, 'shard', split_axis=0, concat_axis=0, tiled=True)]
    convert_element_type x0 -> x1, local copies, waits for them, and re-layouts: none -> 16.2 us  [local(): blocks = jnp.dot(choose.astype(jnp.bfloat16), passages.reshape(held, pass...]
    dot_general x1 -> x4, matrix products: 5.33 us -> 16.6 us  [the longest x1 7.51 us: local(): jnp.einsum('bit,btd->bid', weight.astype(jnp.bfloat16), blocks, preferred...]
    reshape x5 -> x3, local copies, waits for them, and re-layouts: 12.3 us -> 23.2 us  [the longest x1 16.7 us: local(): blocks = jnp.dot(choose.astype(jnp.bfloat16), passages.reshape(held, pass...]
  transfers between devices with their start and end apart: 5 -> 5, of which waited for: 3 -> 4; matrix products, arithmetic and copies ran while one was open for 13% -> 5% of each run, Pallas kernels for 0% -> 0%
where the time goes in v2:
time: 374 us; the launch traced here: 367 us
  waiting for transfers between devices  111 us (30%)
  local copies, waits for them, and re-layouts  92.1 us (25%)
  other arithmetic  73.2 us (20%)
  matrix products  33.9 us (9%)
  starting transfers between devices  31.1 us (8%)
  blocking collectives  24.3 us (6%)
    all_to_all x1, waiting for transfers between devices, local(): lax.all_to_all(back.reshape(owners, capacity * width), 'shard', 0, 0, til...  52 us
    all_to_all x1, waiting for transfers between devices, local(): lax.all_to_all(payload.reshape(owners, capacity * width), 'shard', 0, 0,...  45.5 us
    unnamed x42, local copies, waits for them, and re-layouts  35.7 us
    all_to_all x2, other arithmetic, local(): lax.all_to_all(payload.reshape(owners, capacity * width), 'shard', 0, 0,...  28.2 us
    all_to_all x2, other arithmetic, local(): lax.all_to_all(back.reshape(owners, capacity * width), 'shard', 0, 0, til...  26.9 us
    all_to_all x1, blocking collectives, spread_sum(): summed = lax.all_to_all(pieces, axis, 0, 0, tiled=True).sum(axis=0)  21.8 us
    reshape x1, local copies, waits for them, and re-layouts, local(): blocks = jnp.dot(choose.astype(jnp.bfloat16), passages.reshape(held, pass...  16.7 us
    convert_element_type x1, local copies, waits for them, and re-layouts, local(): blocks = jnp.dot(choose.astype(jnp.bfloat16), passages.reshape(held, pass...  16.2 us
  transfers between devices with their start and end apart: 5, of which 4 were waited for; matrix products, arithmetic and copies ran while one was open for 5% of the time, Pallas kernels for 0%

profile of v2, /device:TPU:2, one launch (start us, length us, event | category | flops | bytes accessed | tf_op | source)
XLA Modules:
  0.0 367.4 jit_solution(10493434653424980008)
XLA Ops:
  0.6 0.9 copy-done
  1.5 1.1 fusion.7
  2.7 1.5 fusion.26
  4.2 0.5 broadcast.236
  4.7 1.3 reduce.11
  6.5 0.8 broadcast_in_dim.162
  7.3 2.6 fusion.17
  10.3 0.2 and_reduce_fusion
  10.7 0.8 convolution_convert_fusion.1
  11.5 0.2 pad_maximum_fusion
  11.7 6.2 %all_to_all.24 = bf16[128,1,8448]{2,1,0:T(2,128)(2,1)} reshape(bf16[256,4224]{1,0:T(8,128)(2,1)S(1)} %pad_maximum_fusion) | data formatting | bytes 4325376 | tf_op jit(solution)/shard_map/all_to_all | solution.py:110
  17.8 0.5 broadcast.237
  18.3 13.8 %reduce.12 = bf16[128,8448]{1,0:T(8,128)(2,1)S(1)} reduce(bf16[128,1,8448]{2,1,0:T(2,128)(2,1)} %all_to_all.24, bf16[]{:T(256)} %broadcast.237), dimensions={1}, to_apply=%all_to_all.24.reduce_sub_computation | reduce | bytes 4325378 | tf_op jit(solution)/shard_map/all_to_all | solution.py:110
  32.1 2.1 reshape.427
  34.2 16.0 %all-to-all-start = ((bf16[128,2,4224]{2,1,0:T(2,128)(2,1)}), bf16[128,2,4224]{2,1,0:T(2,128)(2,1)S(1)}, u32[]{:S(2)}, u32[]{:S(2)}) async-start(bf16[128,2,4224]{2,1,0:T(2,128)(2,1)} %reshape.427), calls=%async_computation | async-start | bytes 4325376 | tf_op jit(solution)/shard_map/all_to_all | solution.py:110
  50.2 8.4 %copy.36 = bf16[128,180,128]{0,2,1:T(8,128)(2,1)} copy(bf16[128,180,128]{2,0,1:T(8,128)(2,1)} %param.10) | data formatting | bytes 11796480 | tf_op args[2]
  58.7 45.5 %all-to-all-done = bf16[128,2,4224]{2,1,0:T(2,128)(2,1)S(1)} async-done(((bf16[128,2,4224]{2,1,0:T(2,128)(2,1)}), bf16[128,2,4224]{2,1,0:T(2,128)(2,1)S(1)}, u32[]{:S(2)}, u32[]{:S(2)}) %all-to-all-start) | async-done | bytes 2162720 | tf_op jit(solution)/shard_map/all_to_all | solution.py:110
  104.2 6.6 %reshape.428 = bf16[128,1,8448]{2,1,0:T(2,128)(2,1)} reshape(bf16[128,2,4224]{2,1,0:T(2,128)(2,1)S(1)} %all-to-all-done) | data formatting | bytes 4325376
  110.8 14.4 %reduce.1 = bf16[128,8448]{1,0:T(8,128)(2,1)} reduce(bf16[128,1,8448]{2,1,0:T(2,128)(2,1)} %reshape.428, bf16[]{:T(256)} %constant.99), dimensions={1}, to_apply=%all_to_all.19.reduce_sub_computation | reduce | bytes 4325378 | tf_op jit(solution)/shard_map/all_to_all | solution.py:110
  125.3 4.3 %reshape.322 = bf16[256,4224]{1,0:T(8,128)(2,1)} reshape(bf16[128,8448]{1,0:T(8,128)(2,1)} %reduce.1) | data formatting | bytes 4325376 | tf_op jit(solution)/shard_map/reshape | solution.py:112
  129.5 1.1 convert_reduce_fusion
  130.7 1.9 slice_bitcast_fusion.1
  132.6 0.2 select_reduce_fusion.1
  132.9 1.9 copy.43
  134.8 6.2 %convolution_convert_fusion = bf16[256,23040]{1,0:T(8,128)(2,1)} fusion(bf16[128,23040]{0,1:T(8,128)(2,1)S(1)} %bitcast.53, s32[256]{0:T(256)S(1)} %get-tuple-element.26), kind=kOutput, calls=%fused_computation | convolution fusion | flops 1515880448 | bytes 17695744 | tf_op jit(solution)/shard_map/dot_general | solution.py:118
  141.0 16.2 %copy.37 = bf16[256,23040]{0,1:T(8,128)(2,1)} copy(bf16[256,23040]{1,0:T(8,128)(2,1)} %convolution_convert_fusion) | data formatting | bytes 23592960 | tf_op jit(solution)/shard_map/convert_element_type | solution.py:123
  157.2 16.7 %copy.38 = bf16[256,180,128]{2,1,0:T(8,128)(2,1)} copy(bf16[256,180,128]{0,2,1:T(8,128)(2,1)} %bitcast.50) | data formatting | bytes 23592960 | tf_op jit(solution)/shard_map/reshape | solution.py:124
  173.9 15.2 %fusion = (f32[256,32]{1,0:T(8,128)S(1)}, f32[256,32,180]{2,1,0:T(8,128)}) fusion(pred[256,180]{1,0:T(8,128)(4,1)S(1)} %iota_compare_fusion, bf16[256,32,128]{2,1,0:T(8,128)(2,1)S(1)} %bitcast.56, bf16[256,180,128]{2,1,0:T(8,128)(2,1)} %copy.38), kind=kOutput, calls=%fused_computation.4 | convolution fusion | flops 381902848 | bytes 19870720 | tf_op jit(solution)/shard_map/bid,btd->bit/dot_general | solution.py:22
  189.1 7.1 %fusion.1 = f32[256,32]{1,0:T(8,128)S(1)} fusion(f32[256,32,180]{2,1,0:T(8,128)} %get-tuple-element.63, f32[256,32]{1,0:T(8,128)S(1)} %get-tuple-element.62, pred[256,180]{1,0:T(8,128)(4,1)S(1)} %iota_compare_fusion), kind=kLoop, calls=%fused_computation.5 | loop fusion | flops 7364608 | bytes 6009856 | tf_op jit(solution)/shard_map/reduce_sum | solution.py:28
  196.2 7.5 %fusion.5 = bf16[256,32,128]{2,1,0:T(8,128)(2,1)S(1)} fusion(bf16[256,180,128]{2,1,0:T(8,128)(2,1)} %copy.38, f32[256,32,180]{2,1,0:T(8,128)S(1)} %copy-done.1, f32[256,32]{1,0:T(8,128)S(1)} %fusion.1, f32[256,32]{1,0:T(8,128)S(1)} %get-tuple-element.62, pred[256,180]{1,0:T(8,128)(4,1)S(1)} %iota_compare_fusion), kind=kOutput, calls=%fused_computation.16 | convolution fusion | flops 387383296 | bytes 19903488 | tf_op jit(solution)/shard_map/bit,btd->bid/dot_general | solution.py:131
  203.7 0.2 select_reduce_fusion
  203.9 1.0 copy.51
  205.1 0.2 pad_maximum_fusion.1
  205.3 6.2 %all_to_all.25 = bf16[128,1,8448]{2,1,0:T(2,128)(2,1)} reshape(bf16[256,4224]{1,0:T(8,128)(2,1)S(1)} %pad_maximum_fusion.1) | data formatting | bytes 4325376 | tf_op jit(solution)/shard_map/all_to_all | solution.py:138
  211.4 13.8 %reduce.13 = bf16[128,8448]{1,0:T(8,128)(2,1)S(1)} reduce(bf16[128,1,8448]{2,1,0:T(2,128)(2,1)} %all_to_all.25, bf16[]{:T(256)} %broadcast.237), dimensions={1}, to_apply=%all_to_all.25.reduce_sub_computation | reduce | bytes 4325378 | tf_op jit(solution)/shard_map/all_to_all | solution.py:138
  225.2 2.1 reshape.429
  227.4 8.2 %all-to-all-start.1 = ((bf16[128,2,4224]{2,1,0:T(2,128)(2,1)}), bf16[128,2,4224]{2,1,0:T(2,128)(2,1)S(1)}, u32[]{:S(2)}, u32[]{:S(2)}) async-start(bf16[128,2,4224]{2,1,0:T(2,128)(2,1)} %reshape.429), calls=%async_computation.1 | async-start | bytes 4325376 | tf_op jit(solution)/shard_map/all_to_all | solution.py:138
  235.7 0.6 dynamic-slice
  236.9 0.2 dynamic-update-slice.1
  237.2 52.0 %all-to-all-done.1 = bf16[128,2,4224]{2,1,0:T(2,128)(2,1)S(1)} async-done(((bf16[128,2,4224]{2,1,0:T(2,128)(2,1)}), bf16[128,2,4224]{2,1,0:T(2,128)(2,1)S(1)}, u32[]{:S(2)}, u32[]{:S(2)}) %all-to-all-start.1) | async-done | bytes 2162720 | tf_op jit(solution)/shard_map/all_to_all | solution.py:138
  289.2 6.5 %reshape.430 = bf16[128,1,8448]{2,1,0:T(2,128)(2,1)} reshape(bf16[128,2,4224]{2,1,0:T(2,128)(2,1)S(1)} %all-to-all-done.1) | data formatting | bytes 4325376
  295.8 13.1 %reduce.4 = bf16[128,8448]{1,0:T(8,128)(2,1)S(1)} reduce(bf16[128,1,8448]{2,1,0:T(2,128)(2,1)} %reshape.430, bf16[]{:T(256)} %constant.99), dimensions={1}, to_apply=%all_to_all.21.reduce_sub_computation | reduce | bytes 4325378 | tf_op jit(solution)/shard_map/all_to_all | solution.py:138
  308.9 2.3 reshape.327
  311.1 2.1 fusion.6
  313.3 0.2 fusion.9
  313.4 0.2 slice_bitcast_fusion
  313.9 0.2 multiply_reduce_fusion.2
  314.1 0.2 dynamic-update-slice.3
  314.3 0.2 dynamic-update-slice.4
  314.6 0.2 dynamic-update-slice.2
  314.8 0.2 dynamic-update-slice
  315.0 1.7 copy.45
  316.7 2.4 all-reduce.5
  319.1 0.6 subtract_add_fusion
  319.8 1.8 fusion.4
  321.7 0.3 collective-permute-start.1
  322.0 1.1 collective-permute-done.1
  323.4 0.2 convolution_bitcast_fusion
  323.8 21.8 %all_to_all.30 = f32[128,3,128]{2,1,0:T(4,128)S(1)} all-to-all(f32[128,3,128]{2,1,0:T(4,128)S(1)} %reshape.331), channel_id=1, replica_groups=mesh['section'=2,'shard'=128] {'shard'}, dimensions={0} | all-to-all | bytes 393216 | tf_op jit(solution)/shard_map/all_to_all | solution.py:55
  345.8 0.7 broadcast_in_dim.176
  346.5 6.6 %all-to-all-start.3 = ((f32[128,3,128]{2,1,0:T(4,128)}), f32[128,3,128]{2,1,0:T(4,128)S(1)}, u32[]{:S(2)}, u32[]{:S(2)}) async-start(f32[128,3,128]{2,1,0:T(4,128)} %broadcast_in_dim.176), calls=%async_computation.3 | async-start | bytes 524288 | tf_op jit(solution)/shard_map/all_to_all | solution.py:57
  353.1 0.8 convolution_convert_fusion.2
  353.9 12.5 %all-to-all-done.3 = f32[128,3,128]{2,1,0:T(4,128)S(1)} async-done(((f32[128,3,128]{2,1,0:T(4,128)}), f32[128,3,128]{2,1,0:T(4,128)S(1)}, u32[]{:S(2)}, u32[]{:S(2)}) %all-to-all-start.3) | async-done | bytes 196640 | tf_op jit(solution)/shard_map/all_to_all | solution.py:57
  366.4 0.8 reshape.332
  (58 shorter events, 2.7 us)
Async XLA Ops:
  0.6 0.9 copy-start
  2.6 7.9 %collective-permute-start = (f32[4,32,128]{2,1,0:T(8,128)S(1)}, f32[4,32,128]{2,1,0:T(8,128)S(1)}, u32[]{:S(2)}, u32[]{:S(2)}) collective-permute-start(f32[4,32,128]{2,1,0:T(8,128)S(1)} %fusion.7), channel_id=1, source_target_pairs={{0,128},{128,0},{1,129},{129,1},{2,130},{130,2},{3,131},{131,3},{4... | collective-permute-start | bytes 196616 | tf_op jit(solution)/shard_map/ppermute | solution.py:50
  34.2 70.0 %all-to-all-start = ((bf16[128,2,4224]{2,1,0:T(2,128)(2,1)}), bf16[128,2,4224]{2,1,0:T(2,128)(2,1)S(1)}, u32[]{:S(2)}, u32[]{:S(2)}) async-start(bf16[128,2,4224]{2,1,0:T(2,128)(2,1)} %reshape.427), calls=%async_computation | async-start | bytes 4325376 | tf_op jit(solution)/shard_map/all_to_all | solution.py:110
  125.3 7.3 %copy-start.6 = (s32[128]{0:T(128)S(1)}, s32[128]{0:T(128)}, u32[]{:S(2)}) copy-start(s32[128]{0:T(128)} %param.11) | copy-start | bytes 1540
  125.3 9.5 %slice-start = ((s8[5898240]{0:T(1024)(128)(4,1)}), s8[1703936]{0:T(1024)(128)(4,1)S(1)}, s32[]{:S(2)}) async-start(s8[5898240]{0:T(1024)(128)(4,1)} %bitcast.51), calls=%async_computation.4 | async-start | bytes 3407872
  130.7 4.1 %slice-start.1 = ((s8[5898240]{0:T(1024)(128)(4,1)}), s8[4194304]{0:T(1024)(128)(4,1)S(1)}, s32[]{:S(2)}) async-start(s8[5898240]{0:T(1024)(128)(4,1)} %bitcast.51), calls=%async_computation.5 | async-start | bytes 8388608
  157.2 16.7 %copy-start.2 = (bf16[32,8,32,128]{3,2,1,0:T(8,128)(2,1)S(1)}, bf16[32,8,32,128]{3,2,1,0:T(8,128)(2,1)}, u32[]{:S(2)}) copy-start(bf16[32,8,32,128]{3,2,1,0:T(8,128)(2,1)} %copy.43) | copy-start | bytes 6291460
  189.1 7.1 %copy-start.1 = (f32[256,32,180]{2,1,0:T(8,128)S(1)}, f32[256,32,180]{2,1,0:T(8,128)}, u32[]{:S(2)}) copy-start(f32[256,32,180]{2,1,0:T(8,128)} %get-tuple-element.63) | copy-start | bytes 17694724
  225.2 10.3 %copy-start.4 = (f32[4,32]{1,0:T(4,128)S(1)}, f32[4,32]{1,0:T(4,128)}, u32[]{:S(2)}) copy-start(f32[4,32]{1,0:T(4,128)} %param.15) | copy-start | bytes 1540
  225.2 10.5 %copy-start.7 = (u32[256]{0:T(256)S(1)}, u32[256]{0:T(256)}, u32[]{:S(2)}) copy-start(u32[256]{0:T(256)} %constant.70) | copy-start | bytes 3076
  225.2 11.9 %copy-start.5 = (s32[4]{0:T(128)S(1)}, s32[4]{0:T(128)}, u32[]{:S(2)}) copy-start(s32[4]{0:T(128)} %param.12) | copy-start | bytes 52
  227.4 61.8 %all-to-all-start.1 = ((bf16[128,2,4224]{2,1,0:T(2,128)(2,1)}), bf16[128,2,4224]{2,1,0:T(2,128)(2,1)S(1)}, u32[]{:S(2)}, u32[]{:S(2)}) async-start(bf16[128,2,4224]{2,1,0:T(2,128)(2,1)} %reshape.429), calls=%async_computation.1 | async-start | bytes 4325376 | tf_op jit(solution)/shard_map/all_to_all | solution.py:138
  315.0 38.1 %copy-start.3 = (bf16[384,128]{1,0:T(8,128)(2,1)S(1)}, bf16[384,128]{1,0:T(8,128)(2,1)}, u32[]{:S(2)}) copy-start(bf16[384,128]{1,0:T(8,128)(2,1)} %param.9) | copy-start | bytes 294916
  321.7 1.3 collective-permute-start.1
  346.5 19.9 %all-to-all-start.3 = ((f32[128,3,128]{2,1,0:T(4,128)}), f32[128,3,128]{2,1,0:T(4,128)S(1)}, u32[]{:S(2)}, u32[]{:S(2)}) async-start(f32[128,3,128]{2,1,0:T(4,128)} %broadcast_in_dim.176), calls=%async_computation.3 | async-start | bytes 524288 | tf_op jit(solution)/shard_map/all_to_all | solution.py:57
